TPU v7x, 256 devices: a whole 4x4x8 slice. The times are simulated.
256 devices in a mesh: spot: 16 (over x, y_hi, core), gene: 16 (over y_lo, z).
Axes of the slice: x: 4, y: 4 (y_hi: 2, y_lo: 2; y = y_hi * 2 + y_lo), z: 8, core: 2. Of those that a mesh axis runs over, the one named last changes fastest.
Arguments:
- counts: int32 [64, 512, 4096], P('spot', None, 'gene'), may hold values from 0 to 56, as said below
- tissue: int32 [64, 512], P('spot'), may hold values from 0 to 1
- tile_ids: int32 [64, 512], P('spot'), may hold values from 0 to 32767, as said below
Outputs:
- statistic: float32 [4096, 4096], P('gene', 'spot')
Inputs may be any that keep to these rules, and one draw needn't show every extreme that they name: `counts`: whole numbers of molecules. `tile_ids`: bins of one tile form a rectangle of the grid; tiles are bands of rows crossed with bands of columns.
All inputs are finite; a program needn't handle non-finite values.
Results may differ from a plain program's by a relative error of at most 0.003.
Values may be sent and summed in bfloat16 or wider, within the bound.
No kernel may reach another device: no remote copies, remote signals or barrier semaphores. Data moves between devices by JAX's collectives and lax.ppermute only.
A program may use at most 64 MiB of HBM per device.

v0:
```python
import jax
import jax.numpy as jnp
from jax import lax
from jax.sharding import PartitionSpec as P

stencil_taps = [
    (row_off, col_off, 1.0 / (row_off * row_off + col_off * col_off))
    for row_off in range(-2, 3)
    for col_off in range(-2, 3)
    if row_off != 0 or col_off != 0
]
contract_bins = (((0,), (0,)), ((), ()))


def padded(cells, sides, width):
    for axis, dim in sides:
        count = lax.axis_size(axis)
        ends = count - 1
        head = lax.slice_in_dim(cells, 0, width, axis=dim)
        tail = lax.slice_in_dim(cells, cells.shape[dim] - width, cells.shape[dim], axis=dim)
        cells = jnp.concatenate(
            [
                lax.ppermute(tail, axis, [(i, (i + 1) % count) for i in range(ends)]),
                cells,
                lax.ppermute(head, axis, [((i + 1) % count, i) for i in range(ends)]),
            ],
            axis=dim,
        )
    return cells


def cross_panel(left, right):
    return lax.dot_general(left, right, contract_bins, preferred_element_type=jnp.float32)


def shards(counts, tissue, tile_ids):
    row_count, col_count, panel_width = counts.shape
    tile_code = tile_ids * 2 + tissue
    code_rims = padded(tile_code, (("spot", 0),), 2)
    code_wide = jnp.pad(code_rims, ((0, 0), (2, 2)))
    tissue_wide = (code_wide % 2).astype(jnp.float32)
    ids_wide = code_wide // 2
    in_tissue = tissue.astype(jnp.float32)
    weight_sq = jnp.zeros((row_count, col_count), jnp.float32)
    same_list = []
    for row_off, col_off, weight in stencil_taps:
        near_ids = ids_wide[
            2 + row_off : 2 + row_off + row_count, 2 + col_off : 2 + col_off + col_count
        ]
        near_tissue = tissue_wide[
            2 + row_off : 2 + row_off + row_count, 2 + col_off : 2 + col_off + col_count
        ]
        same_tile = (near_ids == tile_ids).astype(jnp.float32)
        weight_sq = weight_sq + weight * weight * same_tile * near_tissue
        same_list.append(same_tile)
    pair_local = jnp.sum(in_tissue * weight_sq)
    count_local = jnp.sum(in_tissue)
    values = counts.astype(jnp.float32)
    masked = values * in_tissue[:, :, None]
    first_sums = jnp.sum(masked, axis=(0, 1))
    total_first, tissue_count, pair_norm = lax.psum((first_sums, count_local, pair_local), "spot")
    gene_mean = total_first / tissue_count
    centred = (values - gene_mean) * in_tissue[:, :, None]
    variance = lax.psum(jnp.sum(centred * centred, axis=(0, 1)), "spot") / tissue_count
    zscores = (centred / jnp.sqrt(variance + 1e-05)).astype(jnp.bfloat16)
    zscore_rims = padded(zscores, (("spot", 0),), 2)
    zscore_wide = jnp.pad(zscore_rims, ((0, 0), (2, 2), (0, 0)))
    lagged_sum = jnp.zeros(values.shape, jnp.float32)
    for (row_off, col_off, weight), same_tile in zip(stencil_taps, same_list):
        near_z = zscore_wide[
            2 + row_off : 2 + row_off + row_count, 2 + col_off : 2 + col_off + col_count, :
        ]
        lagged_sum = lagged_sum + weight * same_tile[:, :, None] * near_z.astype(jnp.float32)
    lagged = lagged_sum.astype(jnp.bfloat16)
    bin_count = row_count * col_count
    flat_z = zscores.reshape(bin_count, panel_width)
    flat_lag = lagged.reshape(bin_count, panel_width)
    totals = cross_panel(flat_z, lax.all_gather(flat_lag, "gene", axis=1, tiled=True))
    share = lax.psum_scatter(totals, "spot", scatter_dimension=1, tiled=True)
    return share / jnp.sqrt(pair_norm)


def solution(mesh):
    placed = (P("spot", None, "gene"), P("spot", None), P("spot", None))
    return jax.shard_map(
        shards, mesh=mesh, in_specs=placed, out_specs=P("gene", "spot"), check_vma=False
    )
```

profile of v0, /device:TPU:32, one launch (start us, length us, event | category | flops | bytes accessed | tf_op | source)
XLA Modules:
  0.0 425.3 jit_solution(14319070710412826453)
XLA Ops:
  6.5 0.9 multiply_add_fusion
  7.4 1.7 collective-permute-start
  9.2 1.3 collective-permute-start.1
  10.5 1.3 convert_reduce_fusion
  11.8 2.0 multiply_reduce_fusion.1
  13.8 40.1 %all-reduce.3 = (f32[256]{0:T(256)S(1)}, f32[]{:T(128)}) all-reduce(f32[256]{0:T(256)S(1)} %multiply_reduce_fusion.1, f32[]{:T(128)} %convert_reduce_fusion), channel_id=1, replica_groups=mesh['spot'=16,'gene'=16] {'spot'}, use_global_device_ids=true, to_apply=%region_1.2 | all-reduce | flops 257 | bytes 2056 | tf_op jit(solution)/shard_map/psum | solution.py:61
  53.8 0.6 broadcast_divide_fusion.1
  54.5 0.4 multiply_reduce_fusion
  54.9 0.1 add_select_fusion.1
  55.2 0.2 broadcast_select_fusion.19
  55.4 0.7 fusion.14
  56.1 33.8 %all-reduce.2 = (f32[256]{0:T(256)S(1)}, f32[]{:T(128)}) all-reduce(f32[256]{0:T(256)S(1)} %multiply_reduce_fusion, f32[]{:T(128)} %fusion.14), channel_id=1, replica_groups=mesh['spot'=16,'gene'=16] {'spot'}, use_global_device_ids=true, to_apply=%region_5.6 | all-reduce | flops 257 | bytes 2056 | tf_op jit(solution)/shard_map/psum | solution.py:64
  89.9 0.7 add_sqrt_fusion
  90.6 0.4 divide_convert_fusion
  91.0 1.8 collective-permute-start.2
  92.8 1.3 collective-permute-start.3
  94.1 0.2 collective-permute-done.2
  94.3 2.3 collective-permute-done.3
  96.6 0.7 fusion.5
  97.4 12.2 %add_convert_fusion = bf16[4,512,256]{2,1,0:T(8,128)(2,1)} fusion(bf16[4,512,256]{2,1,0:T(8,128)(2,1)S(1)} %divide_convert_fusion, bf16[2,512,256]{2,1,0:T(8,128)(2,1)S(1)} %collective-permute-done.3, bf16[2,512,256]{2,1,0:T(8,128)(2,1)S(1)} %collective-permute-done.2, bf16[8,516,256]{2,1,0:T(8,128)(2,1)S(1)} %fusion.5, f32[4,512]{1,0:T(4,128)S(1)} %get-tuple-element.93, ...), kind=kLoop, calls=%fused_computation.8 | loop fusion | flops 39845888 | bytes 24313856 | tf_op jit(solution)/shard_map/convert_element_type | solution.py:74
  109.7 210.7 %all-gather.2.cloned.1.call-done = bf16[2048,4096]{1,0:T(8,128)(2,1)} async-done(((bf16[2048,256]{1,0:T(8,128)(2,1)}), bf16[2048,4096]{1,0:T(8,128)(2,1)}) %all-gather.2.cloned.1.call-update) | async-done | bytes 16777232 | tf_op jit(solution)/shard_map/all_gather | solution.py:78
  320.3 10.1 %fusion.43 = f32[256,4096]{1,0:T(8,128)} fusion(bf16[2048,256]{1,0:T(8,128)(2,1)S(1)} %bitcast.4, bf16[2048,4096]{1,0:T(8,128)(2,1)} %all-gather.2.cloned.1.call-done), kind=kOutput, calls=%fused_computation.137 | convolution fusion | flops 4294967296 | bytes 22020096 | tf_op jit(solution)/shard_map/dot_general | solution.py:33
  331.1 85.7 %reduce-scatter.2.cloned.1.call-done = f32[256,256]{1,0:T(8,128)} async-done(((f32[256,4096]{1,0:T(8,128)}), f32[256,256]{1,0:T(8,128)}) %reduce-scatter.2.cloned.1.call-update) | async-done | bytes 262160 | tf_op jit(solution)/shard_map/reduce_scatter | solution.py:79
  416.8 1.7 broadcast_divide_fusion
  (17 shorter events, 0.3 us)
Async XLA Ops:
  6.5 48.0 %copy-start = (s32[4,512,256]{2,1,0:T(8,128)S(1)}, s32[4,512,256]{2,1,0:T(8,128)}, u32[]{:S(2)}) copy-start(s32[4,512,256]{2,1,0:T(8,128)} %param.3) | copy-start | bytes 6291460
  6.5 313.8 %all-gather.2.cloned.1.call-start = ((), (), s32[]{:S(2)}) async-start(), calls=%async_computation.1 | async-start | bytes 17825792 | tf_op jit(solution)/shard_map/all_gather | solution.py:78
  7.4 47.5 %collective-permute-start = (s32[2,512]{1,0:T(2,128)S(1)}, s32[2,512]{1,0:T(2,128)S(1)}, u32[]{:S(2)}, u32[]{:S(2)}) collective-permute-start(s32[2,512]{1,0:T(2,128)S(1)} %get-tuple-element.103), channel_id=1, source_target_pairs={{0,16},{16,32},{32,48},{48,64},{64,80},{80,96},{96,112},{112,128},... | collective-permute-start | bytes 12296 | tf_op jit(solution)/shard_map/ppermute | solution.py:23
  9.2 45.7 %collective-permute-start.1 = (s32[2,512]{1,0:T(2,128)S(1)}, s32[2,512]{1,0:T(2,128)S(1)}, u32[]{:S(2)}, u32[]{:S(2)}) collective-permute-start(s32[2,512]{1,0:T(2,128)S(1)} %get-tuple-element.104), channel_id=1, source_target_pairs={{16,0},{32,16},{48,32},{64,48},{80,64},{96,80},{112,96},{128,112},... | collective-permute-start | bytes 12296 | tf_op jit(solution)/shard_map/ppermute | solution.py:25
  11.8 43.2 %copy-start.1 = (s32[4,512]{1,0:T(4,128)S(1)}, s32[4,512]{1,0:T(4,128)}, u32[]{:S(2)}) copy-start(s32[4,512]{1,0:T(4,128)} %param.5) | copy-start | bytes 24580
  11.8 43.6 %copy-start.2 = (s32[4,512]{1,0:T(4,128)S(1)}, s32[4,512]{1,0:T(4,128)}, u32[]{:S(2)}) copy-start(s32[4,512]{1,0:T(4,128)} %param.4) | copy-start | bytes 24580
  91.0 3.3 collective-permute-start.2
  92.8 3.8 collective-permute-start.3
  109.6 307.2 %reduce-scatter.2.cloned.1.call-start = ((), (), s32[]{:S(2)}) async-start(), calls=%async_computation.2 | async-start | bytes 4456448 | tf_op jit(solution)/shard_map/reduce_scatter | solution.py:79
Sparse Core Ops, SparseCore 0:
  109.8 210.5 all-gather.1
  330.6 86.1 reduce-scatter.1
where the time goes:
time: 426 us; the launch traced here: 425 us
  waiting for transfers between devices  299 us (70%)
  blocking collectives  73.8 us (17%)
  other arithmetic  22 us (5%)
  between operations  14.1 us (3%)
  matrix products  10.1 us (2%)
  starting transfers between devices  6.18 us (1%)
    all_gather x1, waiting for transfers between devices, shards(): lax.all_gather(flat_lag, 'gene', axis=1, tiled=True)  211 us
    reduce_scatter x1, waiting for transfers between devices, shards(): share = lax.psum_scatter(totals, 'spot', scatter_dimension=1, tiled=True)  85.7 us
    psum x1, blocking collectives, shards(): lax.psum((first_sums, count_local, pair_local), 'spot')  40.1 us
    psum x1, blocking collectives, shards(): lax.psum(jnp.sum(centred * centred, axis=(0, 1)), 'spot') / tissue_count  33.8 us
    convert_element_type x1, other arithmetic, shards(): lagged = lagged_sum.astype(jnp.bfloat16)  12.2 us
    dot_general x1, matrix products, cross_panel(): lax.dot_general(left, right, contract_bins, preferred_element_type=jnp.fl...  10.1 us
  transfers between devices with their start and end apart: 6, of which 4 were waited for; matrix products, arithmetic and copies ran while one was open for 1% of the time, Pallas kernels for 0%

commit v1 on v0

--- a/solution.py
+++ b/solution.py
@@ -61,7 +61,10 @@
     total_first, tissue_count, pair_norm = lax.psum((first_sums, count_local, pair_local), "spot")
     gene_mean = total_first / tissue_count
     centred = (values - gene_mean) * in_tissue[:, :, None]
-    variance = lax.psum(jnp.sum(centred * centred, axis=(0, 1)), "spot") / tissue_count
+    variance = (
+        jnp.sum(lax.all_gather(jnp.sum(centred * centred, axis=(0, 1)), "spot"), axis=0)
+        / tissue_count
+    )
     zscores = (centred / jnp.sqrt(variance + 1e-05)).astype(jnp.bfloat16)
     zscore_rims = padded(zscores, (("spot", 0),), 2)
     zscore_wide = jnp.pad(zscore_rims, ((0, 0), (2, 2), (0, 0)))

time: 426 us -> 414 us (0.972)
  blocking collectives: 73.8 us -> 56.9 us
  waiting for transfers between devices: 299 us -> 304 us
    psum x1 -> x0, blocking collectives: 33.8 us -> none  [shards(): lax.psum(jnp.sum(centred * centred, axis=(0, 1)), 'spot') / tissue_count]
    all_gather x0 -> x1, blocking collectives: none -> 19 us  [shards(): lax.all_gather(jnp.sum(centred * centred, axis=(0, 1)), 'spot')]
    ppermute x2, waiting for transfers between devices: 2.32 us -> 7.24 us  [padded(): lax.ppermute(head, axis, [((i + 1) % count, i) for i in range(ends)])]
  transfers between devices with their start and end apart: 6 -> 6, of which waited for: 4 -> 5; matrix products, arithmetic and copies ran while one was open for 1% -> 1% of each run, Pallas kernels for 0% -> 0%
where the time goes in v1:
time: 414 us
  waiting for transfers between devices  304 us (73%)
  blocking collectives  56.9 us (14%)
  other arithmetic  21.4 us (5%)
  between operations  14.2 us (3%)
  matrix products  10.1 us (2%)
  starting transfers between devices  6.65 us (2%)
    all_gather x1, waiting for transfers between devices, shards(): lax.all_gather(flat_lag, 'gene', axis=1, tiled=True)  211 us
    reduce_scatter x1, waiting for transfers between devices, shards(): share = lax.psum_scatter(totals, 'spot', scatter_dimension=1, tiled=True)  85.7 us
    psum x1, blocking collectives, shards(): lax.psum((first_sums, count_local, pair_local), 'spot')  37.9 us
    all_gather x1, blocking collectives, shards(): lax.all_gather(jnp.sum(centred * centred, axis=(0, 1)), 'spot')  19 us
    convert_element_type x1, other arithmetic, shards(): lagged = lagged_sum.astype(jnp.bfloat16)  12.2 us
    dot_general x1, matrix products, cross_panel(): lax.dot_general(left, right, contract_bins, preferred_element_type=jnp.fl...  10.1 us
  transfers between devices with their start and end apart: 6, of which 5 were waited for; matrix products, arithmetic and copies ran while one was open for 1% of the time, Pallas kernels for 0%

profile of v1, /device:TPU:32, one launch (start us, length us, event | category | flops | bytes accessed | tf_op | source)
XLA Modules:
  0.0 413.6 jit_solution(17210579529651404349)
XLA Ops:
  6.5 0.9 multiply_add_fusion
  7.4 1.7 collective-permute-start
  9.2 1.3 collective-permute-start.1
  10.5 1.9 multiply_reduce_fusion.1
  12.4 0.6 convert_reduce_fusion
  13.0 2.2 collective-permute-done.1
  15.5 0.2 broadcast_select_fusion.19
  15.7 0.8 fusion.14
  16.4 37.9 %all-reduce.2 = (f32[256]{0:T(256)S(1)}, f32[]{:T(128)}, f32[]{:T(128)}) all-reduce(f32[256]{0:T(256)S(1)} %multiply_reduce_fusion.1, f32[]{:T(128)} %convert_reduce_fusion, f32[]{:T(128)} %fusion.14), channel_id=1, replica_groups=mesh['spot'=16,'gene'=16] {'spot'}, use_global_device_ids=true, to_apply=%region_1.2 | all-reduce | flops 258 | bytes 2064 | tf_op jit(solution)/shard_map/psum | solution.py:61
  54.3 0.6 broadcast_divide_fusion.1
  55.0 0.4 multiply_reduce_fusion
  55.4 19.0 %all-gather.1 = f32[16,1,256]{2,1,0:T(1,128)S(1)} all-gather(f32[1,1,256]{2,1,0:T(1,128)S(1)} %bitcast.7), channel_id=2, replica_groups=mesh['spot'=16,'gene'=16] {'spot'}, dimensions={0}, use_global_device_ids=true | all-gather | bytes 17408 | tf_op jit(solution)/shard_map/all_gather | solution.py:65
  74.4 0.7 add_sqrt_fusion
  75.1 0.4 divide_convert_fusion
  75.5 2.3 collective-permute-start.2
  77.8 1.3 collective-permute-start.3
  79.1 0.2 collective-permute-done.2
  79.3 5.1 %collective-permute-done.3 = bf16[2,512,256]{2,1,0:T(8,128)(2,1)S(1)} collective-permute-done((bf16[2,512,256]{2,1,0:T(8,128)(2,1)S(1)}, bf16[2,512,256]{2,1,0:T(8,128)(2,1)S(1)}, u32[]{:S(2)}, u32[]{:S(2)}) %collective-permute-start.3) | collective-permute-done | bytes 524320 | tf_op jit(solution)/shard_map/ppermute | solution.py:25
  84.4 0.7 fusion.5
  85.1 12.2 %add_convert_fusion = bf16[4,512,256]{2,1,0:T(8,128)(2,1)} fusion(bf16[4,512,256]{2,1,0:T(8,128)(2,1)S(1)} %divide_convert_fusion, bf16[2,512,256]{2,1,0:T(8,128)(2,1)S(1)} %collective-permute-done.3, bf16[2,512,256]{2,1,0:T(8,128)(2,1)S(1)} %collective-permute-done.2, bf16[8,516,256]{2,1,0:T(8,128)(2,1)S(1)} %fusion.5, f32[4,512]{1,0:T(4,128)S(1)} %get-tuple-element.92, ...), kind=kLoop, calls=%fused_computation.8 | loop fusion | flops 39845888 | bytes 24313856 | tf_op jit(solution)/shard_map/convert_element_type | solution.py:77
  97.4 211.2 %all-gather.4.cloned.1.call-done = bf16[2048,4096]{1,0:T(8,128)(2,1)} async-done(((bf16[2048,256]{1,0:T(8,128)(2,1)}), bf16[2048,4096]{1,0:T(8,128)(2,1)}) %all-gather.4.cloned.1.call-update) | async-done | bytes 16777232 | tf_op jit(solution)/shard_map/all_gather | solution.py:81
  308.6 10.1 %fusion.43 = f32[256,4096]{1,0:T(8,128)} fusion(bf16[2048,256]{1,0:T(8,128)(2,1)S(1)} %bitcast.5, bf16[2048,4096]{1,0:T(8,128)(2,1)} %all-gather.4.cloned.1.call-done), kind=kOutput, calls=%fused_computation.137 | convolution fusion | flops 4294967296 | bytes 22020096 | tf_op jit(solution)/shard_map/dot_general | solution.py:33
  319.4 85.7 %reduce-scatter.2.cloned.1.call-done = f32[256,256]{1,0:T(8,128)} async-done(((f32[256,4096]{1,0:T(8,128)}), f32[256,256]{1,0:T(8,128)}) %reduce-scatter.2.cloned.1.call-update) | async-done | bytes 262160 | tf_op jit(solution)/shard_map/reduce_scatter | solution.py:82
  405.1 1.7 broadcast_divide_fusion
  (18 shorter events, 0.5 us)
Async XLA Ops:
  6.5 8.8 %copy-start.1 = (s32[4,512]{1,0:T(4,128)S(1)}, s32[4,512]{1,0:T(4,128)}, u32[]{:S(2)}) copy-start(s32[4,512]{1,0:T(4,128)} %param.5) | copy-start | bytes 24580
  6.5 5.9 %copy-start.2 = (s32[4,512]{1,0:T(4,128)S(1)}, s32[4,512]{1,0:T(4,128)}, u32[]{:S(2)}) copy-start(s32[4,512]{1,0:T(4,128)} %param.4) | copy-start | bytes 24580
  6.5 48.5 %copy-start = (s32[4,512,256]{2,1,0:T(8,128)S(1)}, s32[4,512,256]{2,1,0:T(8,128)}, u32[]{:S(2)}) copy-start(s32[4,512,256]{2,1,0:T(8,128)} %param.3) | copy-start | bytes 6291460
  6.5 302.1 %all-gather.4.cloned.1.call-start = ((), (), s32[]{:S(2)}) async-start(), calls=%async_computation.1 | async-start | bytes 17825792 | tf_op jit(solution)/shard_map/all_gather | solution.py:81
  7.4 5.6 %collective-permute-start = (s32[2,512]{1,0:T(2,128)S(1)}, s32[2,512]{1,0:T(2,128)S(1)}, u32[]{:S(2)}, u32[]{:S(2)}) collective-permute-start(s32[2,512]{1,0:T(2,128)S(1)} %get-tuple-element.102), channel_id=1, source_target_pairs={{0,16},{16,32},{32,48},{48,64},{64,80},{80,96},{96,112},{112,128},... | collective-permute-start | bytes 12296 | tf_op jit(solution)/shard_map/ppermute | solution.py:23
  9.2 6.0 %collective-permute-start.1 = (s32[2,512]{1,0:T(2,128)S(1)}, s32[2,512]{1,0:T(2,128)S(1)}, u32[]{:S(2)}, u32[]{:S(2)}) collective-permute-start(s32[2,512]{1,0:T(2,128)S(1)} %get-tuple-element.103), channel_id=1, source_target_pairs={{16,0},{32,16},{48,32},{64,48},{80,64},{96,80},{112,96},{128,112},... | collective-permute-start | bytes 12296 | tf_op jit(solution)/shard_map/ppermute | solution.py:25
  75.5 3.8 collective-permute-start.2
  77.8 6.5 %collective-permute-start.3 = (bf16[2,512,256]{2,1,0:T(8,128)(2,1)S(1)}, bf16[2,512,256]{2,1,0:T(8,128)(2,1)S(1)}, u32[]{:S(2)}, u32[]{:S(2)}) collective-permute-start(bf16[2,512,256]{2,1,0:T(8,128)(2,1)S(1)} %get-tuple-element.57), channel_id=1, source_target_pairs={{16,0},{32,16},{48,32},{64,48},{80,64},{96,80},{112,96},{128,112},... | collective-permute-start | bytes 1572872 | tf_op jit(solution)/shard_map/ppermute | solution.py:25
  97.4 307.7 %reduce-scatter.2.cloned.1.call-start = ((), (), s32[]{:S(2)}) async-start(), calls=%async_computation.2 | async-start | bytes 4456448 | tf_op jit(solution)/shard_map/reduce_scatter | solution.py:82
Sparse Core Ops, SparseCore 0:
  97.5 211.0 all-gather.3
  318.9 86.1 reduce-scatter.1
